TPU v7x, 256 devices: a whole 4x4x8 slice. The times are simulated.
256 devices in a mesh: ta: 8 (over x_lo, y), gx: 4 (over x_hi, core), yz: 8 (over z).
Axes of the slice: x: 4 (x_hi: 2, x_lo: 2; x = x_hi * 2 + x_lo), y: 4, z: 8, core: 2. Of those that a mesh axis runs over, the one named last changes fastest.
Arguments:
- vectors: bfloat16 [2, 3, 32, 64, 256, 128], P(None, None, 'gx', 'yz', 'ta'), parts along dimension 4, may hold values from -6 to 6
- gauge_x: float32 [2, 3, 3, 32, 64, 256], P(None, None, None, 'gx', 'yz', 'ta'), parts along dimension 5, may hold values from -6 to 6
- gauge_y: float32 [2, 3, 3, 32, 64, 256], P(None, None, None, 'gx', 'yz', 'ta'), parts along dimension 5, may hold values from -6 to 6
Outputs:
- elementals: float32 [16, 2, 128, 128], P('ta'), parts along dimension 0
There are 8 independent parts, one for each index of `ta`. A program takes and returns all parts, laid end to end along the dimension named above; each array names one. Nothing has to cross between parts.
All inputs are finite; a program needn't handle non-finite values.
Results may differ from a plain program's by a relative error of at most 0.0029.
Values may be sent and summed in bfloat16 or wider, within the bound.
No kernel may reach another device: no remote copies, remote signals or barrier semaphores. Data moves between devices by JAX's collectives and lax.ppermute only.
A program may use at most 64 MiB of HBM per device.

v0:
```python
import math
import jax
import jax.numpy as jnp
from jax import lax
from jax.sharding import PartitionSpec as P


def shifted(value, axis, steps):
    count = lax.axis_size(axis)
    pairs = [(source, (source + steps) % count) for source in range(count)]
    return lax.ppermute(value, axis, pairs)


def colour_apply(gauge, source_vectors):
    real_parts = []
    imag_parts = []
    for colour in range(3):
        real_running = jnp.zeros(source_vectors.shape[2:], jnp.float32)
        imaginary_running = jnp.zeros(source_vectors.shape[2:], jnp.float32)
        for inner_product in range(3):
            left_real = gauge[0, colour, inner_product][..., None]
            left_imaginary = gauge[1, colour, inner_product][..., None]
            right_real = source_vectors[0, inner_product].astype(jnp.float32)
            right_imaginary = source_vectors[1, inner_product].astype(jnp.float32)
            real_running = real_running + left_real * right_real - left_imaginary * right_imaginary
            imaginary_running = (
                imaginary_running + left_real * right_imaginary + left_imaginary * right_real
            )
        real_parts.append(real_running)
        imag_parts.append(imaginary_running)
    return jnp.stack([jnp.stack(real_parts), jnp.stack(imag_parts)]).astype(jnp.bfloat16)


def right_block(image):
    nvecs = image.shape[-1]
    real_rows = image[0].reshape(-1, nvecs)
    imag_rows = image[1].reshape(-1, nvecs)
    first = jnp.concatenate([real_rows, imag_rows], 0)
    second = jnp.concatenate([imag_rows, -real_rows], 0)
    return (first, second)


def contract(left_cols, right_cols):
    return lax.dot_general(
        left_cols, right_cols, (((0,), (0,)), ((), ())), preferred_element_type=jnp.float32
    )


def local(vectors, gauge_x, gauge_y):
    nvecs = vectors.shape[-1]
    from_next_x = shifted(vectors[:, :, :1], "gx", -1)
    shifted_x = jnp.concatenate([vectors[:, :, 1:], from_next_x], 2)
    from_next_y = shifted(vectors[:, :, :, :1], "yz", -1)
    shifted_y = jnp.concatenate([vectors[:, :, :, 1:], from_next_y], 3)
    image_x = colour_apply(gauge_x, shifted_x)
    image_y = colour_apply(gauge_y, shifted_y)
    left_rows = vectors.reshape(-1, nvecs)
    blocks = right_block(image_x) + right_block(image_y)
    summed = lax.psum(
        jnp.concatenate([contract(left_rows, member) for member in blocks], 1), ("gx", "yz")
    )
    sites_total = (
        vectors.shape[2]
        * lax.axis_size("gx")
        * vectors.shape[3]
        * lax.axis_size("yz")
        * vectors.shape[4]
    )
    scaling = 1.0 / math.sqrt(3.0 * sites_total)
    return (summed * scaling).reshape(nvecs, 2, 2, nvecs).transpose(1, 2, 0, 3)


def solution(mesh):
    placed = (
        P(None, None, "gx", "yz", "ta", None),
        P(None, None, None, "gx", "yz", "ta"),
        P(None, None, None, "gx", "yz", "ta"),
    )
    return jax.shard_map(
        local, mesh=mesh, in_specs=placed, out_specs=P("ta", None, None, None), check_vma=False
    )
```

profile of v0, /device:TPU:8, one launch (start us, length us, event | category | flops | bytes accessed | tf_op | source)
XLA Modules:
  0.0 315.3 jit_solution(16234775033811610859)
XLA Ops:
  6.5 0.0 all-reduce.2.cloned.1.call-start
  6.5 1.0 slice.186
  7.6 0.0 copy-start
  7.6 2.5 collective-permute-start
  10.1 1.0 slice.212
  11.1 5.9 %collective-permute-start.1 = (bf16[2,3,8,1,32,128]{5,4,3,2,1,0:T(8,128)(2,1)S(1)}, bf16[2,3,8,1,32,128]{5,4,3,2,1,0:T(8,128)(2,1)S(1)}, u32[]{:S(2)}, u32[]{:S(2)}) collective-permute-start(bf16[2,3,8,1,32,128]{5,4,3,2,1,0:T(8,128)(2,1)S(1)} %slice.212), channel_id=1, source_target_pairs={{0,7},{1,0},{2,1},{3,2},{4,3},{5,4},{6,5},{7,6},{8,15},{9,8},{10,9... | collective-permute-start | bytes 1179656 | tf_op jit(solution)/shard_map/ppermute | solution.py:11
  17.1 0.0 copy-done
  17.1 0.0 copy-start.1
  17.1 0.0 copy-start.2
  17.1 0.0 slice-start
  17.1 0.7 slice.211
  17.8 0.4 copy-done.1
  18.2 0.1 copy-done.2
  18.4 0.0 collective-permute-done
  18.4 0.8 slice-done
  19.2 2.1 fusion.51
  21.3 1.9 fusion.33
  23.3 3.9 %fusion.57 = (bf16[1,8,8,32,128]{4,3,2,1,0:T(8,128)(2,1)S(1)}, bf16[1,8,8,32,128]{4,3,2,1,0:T(8,128)(2,1)S(1)}, bf16[1,8,8,32,128]{4,3,2,1,0:T(8,128)(2,1)S(1)}, bf16[1,8,8,32,128]{4,3,2,1,0:T(8,128)(2,1)S(1)}) fusion(bf16[1,8,8,32,128]{4,3,2,1,0:T(8,128)(2,1)S(1)} %get-tuple-element.11, bf16[1,8,8,32,128]{4,3,2,1,0:T(8,128)(2,1)S(1)} %get-tuple-element.10, ...), kind=kLoop, calls=%fused_computation.145 | loop fusion | flops 14155776 | bytes 5341184 | tf_op jit(solution)/shard_map/convert.26
  27.2 0.3 pad_maximum_fusion
  27.5 0.3 bitcast_negate_fusion.1
  27.8 1.0 fusion.25
  28.9 1.0 fusion.22
  29.9 0.0 collective-permute-done.1
  29.9 2.0 fusion.87
  31.9 1.9 fusion.69
  33.9 3.9 %fusion.93 = (bf16[1,8,8,32,128]{4,3,2,1,0:T(8,128)(2,1)S(1)}, bf16[1,8,8,32,128]{4,3,2,1,0:T(8,128)(2,1)S(1)}, bf16[1,8,8,32,128]{4,3,2,1,0:T(8,128)(2,1)S(1)}, bf16[1,8,8,32,128]{4,3,2,1,0:T(8,128)(2,1)S(1)}) fusion(bf16[1,8,8,32,128]{4,3,2,1,0:T(8,128)(2,1)S(1)} %get-tuple-element.18, bf16[1,8,8,32,128]{4,3,2,1,0:T(8,128)(2,1)S(1)} %get-tuple-element.17, ...), kind=kLoop, calls=%fused_computation.181 | loop fusion | flops 14155776 | bytes 5341184 | tf_op jit(solution)/shard_map/convert.16
  37.8 0.3 pad_maximum_fusion.2
  38.2 0.3 bitcast_negate_fusion
  38.5 1.0 fusion.19
  39.5 1.1 fusion.16
  40.6 0.7 pad_maximum_fusion.6
  41.3 0.0 all-reduce.2.cloned.1.call-update
  41.3 265.3 %all-reduce.2.cloned.1.call-done = f32[128,512]{0,1:T(8,128)} async-done(((f32[128,512]{0,1:T(8,128)}), f32[128,512]{0,1:T(8,128)}) %all-reduce.2.cloned.1.call-update) | async-done | bytes 262160 | tf_op jit(solution)/shard_map/psum | solution.py:59
  306.6 1.0 broadcast_multiply_fusion
  307.6 0.8 copy.4
  (2 shorter events, 0.1 us)
Async XLA Ops:
  6.5 300.1 %all-reduce.2.cloned.1.call-start = ((), (), s32[]{:S(2)}) async-start(), calls=%async_computation | async-start | bytes 524288 | tf_op jit(solution)/shard_map/psum | solution.py:59
  7.6 9.5 %copy-start = (bf16[2,3,8,8,32,128]{5,4,3,2,1,0:T(8,128)(2,1)S(1)}, bf16[2,3,8,8,32,128]{5,4,3,2,1,0:T(8,128)(2,1)}, u32[]{:S(2)}) copy-start(bf16[2,3,8,8,32,128]{5,4,3,2,1,0:T(8,128)(2,1)} %param.3) | copy-start | bytes 9437188
  7.6 10.8 %collective-permute-start = (bf16[2,3,1,8,32,128]{5,4,3,2,1,0:T(8,128)(2,1)S(1)}, bf16[2,3,1,8,32,128]{5,4,3,2,1,0:T(8,128)(2,1)S(1)}, u32[]{:S(2)}, u32[]{:S(2)}) collective-permute-start(bf16[2,3,1,8,32,128]{5,4,3,2,1,0:T(8,128)(2,1)S(1)} %slice.186), channel_id=1, source_target_pairs={{0,24},{8,0},{16,8},{24,16},{1,25},{9,1},{17,9},{25,17},{2,26},{10... | collective-permute-start | bytes 1179656 | tf_op jit(solution)/shard_map/ppermute | solution.py:11
  11.1 18.8 %collective-permute-start.1 = (bf16[2,3,8,1,32,128]{5,4,3,2,1,0:T(8,128)(2,1)S(1)}, bf16[2,3,8,1,32,128]{5,4,3,2,1,0:T(8,128)(2,1)S(1)}, u32[]{:S(2)}, u32[]{:S(2)}) collective-permute-start(bf16[2,3,8,1,32,128]{5,4,3,2,1,0:T(8,128)(2,1)S(1)} %slice.212), channel_id=1, source_target_pairs={{0,7},{1,0},{2,1},{3,2},{4,3},{5,4},{6,5},{7,6},{8,15},{9,8},{10,9... | collective-permute-start | bytes 1179656 | tf_op jit(solution)/shard_map/ppermute | solution.py:11
  17.1 1.1 copy-start.1
  17.1 1.2 copy-start.2
  17.1 2.1 slice-start
Sparse Core Ops, SparseCore 0:
  41.5 265.1 all-reduce.1
where the time goes:
time: 315 us
  waiting for transfers between devices  265 us (84%)
  other arithmetic  18.8 us (6%)
  between operations  13.6 us (4%)
  starting transfers between devices  8.47 us (3%)
  local copies, waits for them, and re-layouts  5 us (2%)
  matrix products  4.18 us (1%)
    psum x1, waiting for transfers between devices, local(): lax.psum(jnp.concatenate([contract(left_rows, member) for member in block...  265 us
    another operation x6, other arithmetic  15.8 us
    ppermute x2, starting transfers between devices, shifted(): return lax.ppermute(value, axis, pairs)  8.47 us
  transfers between devices with their start and end apart: 3, of which 1 were waited for; matrix products, arithmetic and copies ran while one was open for 4% of the time, Pallas kernels for 0%

commit v1 on v0

--- a/solution.py
+++ b/solution.py
@@ -57,7 +57,7 @@
     left_rows = vectors.reshape(-1, nvecs)
     blocks = right_block(image_x) + right_block(image_y)
     summed = lax.psum(
-        jnp.concatenate([contract(left_rows, member) for member in blocks], 1), ("gx", "yz")
+        lax.psum(jnp.concatenate([contract(left_rows, member) for member in blocks], 1), "gx"), "yz"
     )
     sites_total = (
         vectors.shape[2]

time: 315 us -> 170 us (0.54)
  waiting for transfers between devices: 265 us -> 120 us
    psum x1, waiting for transfers between devices: 265 us -> 45.2 us  [local(): lax.psum(jnp.concatenate([contract(left_rows, member) for member in block...]
    psum x0 -> x1, waiting for transfers between devices: none -> 74.3 us  [local(): lax.psum(lax.psum(jnp.concatenate([contract(left_rows, member) for member...]
  transfers between devices with their start and end apart: 3 -> 4, of which waited for: 1 -> 2; matrix products, arithmetic and copies ran while one was open for 4% -> 7% of each run, Pallas kernels for 0% -> 0%
where the time goes in v1:
time: 170 us
  waiting for transfers between devices  120 us (71%)
  other arithmetic  18.8 us (11%)
  between operations  13.6 us (8%)
  starting transfers between devices  8.52 us (5%)
  local copies, waits for them, and re-layouts  5 us (3%)
  matrix products  4.18 us (2%)
    psum x1, waiting for transfers between devices, local(): lax.psum(lax.psum(jnp.concatenate([contract(left_rows, member) for member...  74.3 us
    psum x1, waiting for transfers between devices, local(): lax.psum(jnp.concatenate([contract(left_rows, member) for member in block...  45.2 us
    another operation x6, other arithmetic  15.8 us
    ppermute x2, starting transfers between devices, shifted(): return lax.ppermute(value, axis, pairs)  8.47 us
    dot_general x4, matrix products, contract(): lax.dot_general(left_cols, right_cols, (((0,), (0,)), ((), ())), preferre...  4.18 us
  transfers between devices with their start and end apart: 4, of which 2 were waited for; matrix products, arithmetic and copies ran while one was open for 7% of the time, Pallas kernels for 0%

profile of v1, /device:TPU:8, one launch (start us, length us, event | category | flops | bytes accessed | tf_op | source)
XLA Modules:
  0.0 169.6 jit_solution(13807874897228020373)
XLA Ops:
  6.5 0.0 all-reduce.3.cloned.1.call-start
  6.5 1.0 slice.186
  7.6 0.0 copy-start
  7.6 2.5 %collective-permute-start = (bf16[2,3,1,8,32,128]{5,4,3,2,1,0:T(8,128)(2,1)S(1)}, bf16[2,3,1,8,32,128]{5,4,3,2,1,0:T(8,128)(2,1)S(1)}, u32[]{:S(2)}, u32[]{:S(2)}) collective-permute-start(bf16[2,3,1,8,32,128]{5,4,3,2,1,0:T(8,128)(2,1)S(1)} %slice.186), channel_id=1, source_target_pairs={{0,24},{8,0},{16,8},{24,16},{1,25},{9,1},{17,9},{25,17},{2,26},{10... | collective-permute-start | bytes 1179656 | tf_op jit(solution)/shard_map/ppermute | solution.py:11
  10.1 1.0 slice.212
  11.1 5.9 %collective-permute-start.1 = (bf16[2,3,8,1,32,128]{5,4,3,2,1,0:T(8,128)(2,1)S(1)}, bf16[2,3,8,1,32,128]{5,4,3,2,1,0:T(8,128)(2,1)S(1)}, u32[]{:S(2)}, u32[]{:S(2)}) collective-permute-start(bf16[2,3,8,1,32,128]{5,4,3,2,1,0:T(8,128)(2,1)S(1)} %slice.212), channel_id=1, source_target_pairs={{0,7},{1,0},{2,1},{3,2},{4,3},{5,4},{6,5},{7,6},{8,15},{9,8},{10,9... | collective-permute-start | bytes 1179656 | tf_op jit(solution)/shard_map/ppermute | solution.py:11
  17.1 0.0 copy-done
  17.1 0.0 copy-start.1
  17.1 0.0 copy-start.2
  17.1 0.0 slice-start
  17.1 0.7 slice.211
  17.8 0.4 copy-done.1
  18.2 0.1 copy-done.2
  18.4 0.0 collective-permute-done
  18.4 0.8 slice-done
  19.2 2.1 %fusion.51 = (bf16[1,8,8,32,128]{4,3,2,1,0:T(8,128)(2,1)S(1)}, bf16[1,8,8,32,128]{4,3,2,1,0:T(8,128)(2,1)S(1)}, bf16[1,8,8,32,128]{4,3,2,1,0:T(8,128)(2,1)S(1)},...) fusion(f32[8,8,32]{2,1,0:T(8,128)S(1)} %get-tuple-element.41, ...), kind=kLoop, calls=%fused_computation.139 | loop fusion | flops 6291456 | bytes 6864896 | tf_op jit(solution)/shard_map/convert.25
  21.3 1.9 %fusion.33 = bf16[1,8,8,32,128]{4,3,2,1,0:T(8,128)(2,1)S(1)} fusion(bf16[1,8,8,32,128]{4,3,2,1,0:T(8,128)(2,1)S(1)} %get-tuple-element.11, bf16[1,8,8,32,128]{4,3,2,1,0:T(8,128)(2,1)S(1)} %get-tuple-element.10, bf16[1,8,8,32,128]{4,3,2,1,0:T(8,128)(2,1)S(1)} %get-tuple-element.9, bf16[1,8,8,32,128]{4,3,2,1,0:T(8,128)(2,1)S(1)} %get-tuple-element.8, ...), kind=kLoop, calls=%fused_computation.121 | loop fusion | flops 4718592 | bytes 3719168 | tf_op jit(solution)/shard_map/convert.29
  23.3 3.9 %fusion.57 = (bf16[1,8,8,32,128]{4,3,2,1,0:T(8,128)(2,1)S(1)}, bf16[1,8,8,32,128]{4,3,2,1,0:T(8,128)(2,1)S(1)}, bf16[1,8,8,32,128]{4,3,2,1,0:T(8,128)(2,1)S(1)}, bf16[1,8,8,32,128]{4,3,2,1,0:T(8,128)(2,1)S(1)}) fusion(bf16[1,8,8,32,128]{4,3,2,1,0:T(8,128)(2,1)S(1)} %get-tuple-element.11, bf16[1,8,8,32,128]{4,3,2,1,0:T(8,128)(2,1)S(1)} %get-tuple-element.10, ...), kind=kLoop, calls=%fused_computation.145 | loop fusion | flops 14155776 | bytes 5341184 | tf_op jit(solution)/shard_map/convert.26
  27.2 0.3 pad_maximum_fusion
  27.5 0.3 bitcast_negate_fusion.1
  27.8 1.0 fusion.25
  28.9 1.0 fusion.22
  29.9 0.0 collective-permute-done.1
  29.9 2.0 %fusion.87 = (bf16[1,8,8,32,128]{4,3,2,1,0:T(8,128)(2,1)S(1)}, bf16[1,8,8,32,128]{4,3,2,1,0:T(8,128)(2,1)S(1)}, bf16[1,8,8,32,128]{4,3,2,1,0:T(8,128)(2,1)S(1)},...) fusion(f32[8,8,32]{2,1,0:T(8,128)S(1)} %get-tuple-element.59, ...), kind=kLoop, calls=%fused_computation.175 | loop fusion | flops 6291456 | bytes 6864896 | tf_op jit(solution)/shard_map/convert.15
  31.9 1.9 %fusion.69 = bf16[1,8,8,32,128]{4,3,2,1,0:T(8,128)(2,1)S(1)} fusion(bf16[1,8,8,32,128]{4,3,2,1,0:T(8,128)(2,1)S(1)} %get-tuple-element.18, bf16[1,8,8,32,128]{4,3,2,1,0:T(8,128)(2,1)S(1)} %get-tuple-element.17, bf16[1,8,8,32,128]{4,3,2,1,0:T(8,128)(2,1)S(1)} %get-tuple-element.16, bf16[1,8,8,32,128]{4,3,2,1,0:T(8,128)(2,1)S(1)} %get-tuple-element.15, ...), kind=kLoop, calls=%fused_computation.157 | loop fusion | flops 4718592 | bytes 3719168 | tf_op jit(solution)/shard_map/convert.19
  33.9 3.9 %fusion.93 = (bf16[1,8,8,32,128]{4,3,2,1,0:T(8,128)(2,1)S(1)}, bf16[1,8,8,32,128]{4,3,2,1,0:T(8,128)(2,1)S(1)}, bf16[1,8,8,32,128]{4,3,2,1,0:T(8,128)(2,1)S(1)}, bf16[1,8,8,32,128]{4,3,2,1,0:T(8,128)(2,1)S(1)}) fusion(bf16[1,8,8,32,128]{4,3,2,1,0:T(8,128)(2,1)S(1)} %get-tuple-element.18, bf16[1,8,8,32,128]{4,3,2,1,0:T(8,128)(2,1)S(1)} %get-tuple-element.17, ...), kind=kLoop, calls=%fused_computation.181 | loop fusion | flops 14155776 | bytes 5341184 | tf_op jit(solution)/shard_map/convert.16
  37.8 0.3 pad_maximum_fusion.2
  38.2 0.3 bitcast_negate_fusion
  38.5 1.0 fusion.19
  39.5 1.1 fusion.16
  40.6 0.7 pad_maximum_fusion.6
  41.3 0.0 all-reduce.3.cloned.1.call-update
  41.3 0.0 all-reduce.5.cloned.1.call-start
  41.4 45.2 %all-reduce.3.cloned.1.call-done = f32[128,512]{0,1:T(8,128)} async-done(((f32[128,512]{0,1:T(8,128)}), f32[128,512]{0,1:T(8,128)}) %all-reduce.3.cloned.1.call-update) | async-done | bytes 262160 | tf_op jit(solution)/shard_map/psum | solution.py:60
  86.6 0.0 all-reduce.5.cloned.1.call-update
  86.6 74.3 %all-reduce.5.cloned.1.call-done = f32[128,512]{0,1:T(8,128)} async-done(((f32[128,512]{0,1:T(8,128)}), f32[128,512]{0,1:T(8,128)}) %all-reduce.5.cloned.1.call-update) | async-done | bytes 262160 | tf_op jit(solution)/shard_map/psum | solution.py:59
  161.0 1.0 broadcast_multiply_fusion
  161.9 0.8 copy.4
  (2 shorter events, 0.1 us)
Async XLA Ops:
  6.5 80.1 %all-reduce.3.cloned.1.call-start = ((), (), s32[]{:S(2)}) async-start(), calls=%async_computation | async-start | bytes 524288 | tf_op jit(solution)/shard_map/psum | solution.py:60
  7.6 9.5 %copy-start = (bf16[2,3,8,8,32,128]{5,4,3,2,1,0:T(8,128)(2,1)S(1)}, bf16[2,3,8,8,32,128]{5,4,3,2,1,0:T(8,128)(2,1)}, u32[]{:S(2)}) copy-start(bf16[2,3,8,8,32,128]{5,4,3,2,1,0:T(8,128)(2,1)} %param.3) | copy-start | bytes 9437188
  7.6 10.8 %collective-permute-start = (bf16[2,3,1,8,32,128]{5,4,3,2,1,0:T(8,128)(2,1)S(1)}, bf16[2,3,1,8,32,128]{5,4,3,2,1,0:T(8,128)(2,1)S(1)}, u32[]{:S(2)}, u32[]{:S(2)}) collective-permute-start(bf16[2,3,1,8,32,128]{5,4,3,2,1,0:T(8,128)(2,1)S(1)} %slice.186), channel_id=1, source_target_pairs={{0,24},{8,0},{16,8},{24,16},{1,25},{9,1},{17,9},{25,17},{2,26},{10... | collective-permute-start | bytes 1179656 | tf_op jit(solution)/shard_map/ppermute | solution.py:11
  11.1 18.8 %collective-permute-start.1 = (bf16[2,3,8,1,32,128]{5,4,3,2,1,0:T(8,128)(2,1)S(1)}, bf16[2,3,8,1,32,128]{5,4,3,2,1,0:T(8,128)(2,1)S(1)}, u32[]{:S(2)}, u32[]{:S(2)}) collective-permute-start(bf16[2,3,8,1,32,128]{5,4,3,2,1,0:T(8,128)(2,1)S(1)} %slice.212), channel_id=1, source_target_pairs={{0,7},{1,0},{2,1},{3,2},{4,3},{5,4},{6,5},{7,6},{8,15},{9,8},{10,9... | collective-permute-start | bytes 1179656 | tf_op jit(solution)/shard_map/ppermute | solution.py:11
  17.1 1.1 copy-start.1
  17.1 1.2 copy-start.2
  17.1 2.1 %slice-start = ((bf16[2,3,8,8,32,128]{5,4,3,2,1,0:T(8,128)(2,1)}), bf16[2,3,7,8,32,128]{5,4,3,2,1,0:T(8,128)(2,1)S(1)}, s32[]{:S(2)}) async-start(bf16[2,3,8,8,32,128]{5,4,3,2,1,0:T(8,128)(2,1)} %param.3), calls=%async_computation.2 | async-start | bytes 5505024 | tf_op jit(solution)/shard_map/slice | solution.py:52
  41.3 119.6 %all-reduce.5.cloned.1.call-start = ((), (), s32[]{:S(2)}) async-start(), calls=%async_computation.1 | async-start | bytes 524288 | tf_op jit(solution)/shard_map/psum | solution.py:59
Sparse Core Ops, SparseCore 0:
  41.5 45.1 all-reduce.2
  89.0 71.8 all-reduce.4
